TPU v7x, 32 devices: a whole 2x2x4 slice. The times are simulated.
32 devices in a mesh: space: 16 (over z, y, x), ray: 2 (over core).
Axes of the slice: x: 2, y: 2, z: 4, core: 2. Of those that a mesh axis runs over, the one named last changes fastest.
Arguments:
- positions: float32 [3, 512, 256], P(None, ('space', 'ray')), may hold values from -1 to 1
- spacing: float32 [512, 256], P(('space', 'ray')), may hold values from 0.003 to 0.03
- assign: int32 [512, 8, 1], P(('space', 'ray')), may hold values from 0 to 15; in each aligned block of 128 rows (0 to 127, 128 to 255, ..., all dimensions but the last counted through in order) at most 12 rows name the same one
- depth_rank: int32 [512, 8], P(('space', 'ray')), may hold values from 0 to 7, each once within a row
- pixel_grad: float32 [3, 512], P(None, ('space', 'ray')), may hold values from -96 to 96
- fourier: float32 [3, 128], replicated, may hold values from -4 to 4
- first_weight: bfloat16 [16, 256, 256], P('space'), may hold values from -0.375 to 0.375
- first_bias: float32 [16, 256], P('space'), may hold values from -3 to 3
- second_weight: bfloat16 [16, 256, 256], P('space'), may hold values from -0.375 to 0.375
- second_bias: float32 [16, 256], P('space'), may hold values from -3 to 3
- head_weight: bfloat16 [16, 4, 256], P('space'), may hold values from -0.375 to 0.375
- head_bias: float32 [16, 4], P('space'), may hold values from -3 to 3
Outputs:
- grad_first: float32 [16, 256, 256], P('space', 'ray')
- grad_second: float32 [16, 256, 256], P('space', 'ray')
- grad_head: float32 [16, 4, 256], P('space')
- grad_first_bias: float32 [16, 256], P('space')
- grad_second_bias: float32 [16, 256], P('space')
- grad_head_bias: float32 [16, 4], P('space')
Inputs may be any that keep to these rules, and one draw needn't show every extreme that they name: `assign`: within the segments of one device (aligned blocks of 128 rows in ray order), no partition is named more than 12 times. `depth_rank`: each ray's row names every place 0 to 7 once.
All inputs are finite; a program needn't handle non-finite values.
Results may differ from a plain program's by a relative error of at most 0.0053.
Values sent between devices are 32-bit elements; how exact they have to be, the bound alone decides.
No kernel may reach another device: no remote copies, remote signals or barrier semaphores. Data moves between devices by JAX's collectives and lax.ppermute only.
A program may use at most 64 MiB of HBM per device.

v0:
```python
import jax
import jax.numpy as jnp
from jax import lax
from jax.sharding import PartitionSpec as P

SEG_LEN = 32
SEGS = 8
two_pi = 6.283185307179586


def silu_slope(value):
    gate = jax.nn.sigmoid(value)
    return gate * (1.0 + value * (1.0 - gate))


def turn_sin_cos(turns):
    quarter = jnp.round(turns * 4.0)
    angle = (turns - quarter * 0.25) * two_pi
    square = angle * angle
    sine = angle * (
        1.0
        + square
        * (
            -1.0 / 6.0
            + square * (1.0 / 120.0 + square * (-1.0 / 5040.0 + square * (1.0 / 362880.0)))
        )
    )
    cosine = 1.0 + square * (
        -0.5
        + square
        * (
            1.0 / 24.0
            + square * (-1.0 / 720.0 + square * (1.0 / 40320.0 + square * (-1.0 / 3628800.0)))
        )
    )
    step = quarter - 4.0 * jnp.floor(quarter * 0.25)
    flip = step >= 2.0
    odd = (step == 1.0) | (step == 3.0)
    sin_out = jnp.where(odd, cosine, sine)
    cos_out = jnp.where(odd, sine, cosine)
    sin_out = jnp.where(flip, -sin_out, sin_out)
    cos_out = jnp.where(flip != odd, -cos_out, cos_out)
    return (sin_out, cos_out)


def encode(samples, fourier):
    turns = (
        samples[:, 0, :, None] * fourier[0]
        + samples[:, 1, :, None] * fourier[1]
        + samples[:, 2, :, None] * fourier[2]
    )
    sine, cosine = turn_sin_cos(turns)
    joined = jnp.concatenate([sine, cosine], axis=-1)
    return joined.astype(jnp.bfloat16).reshape(-1, joined.shape[-1])


def network(samples, fourier, params):
    first_weight, first_bias, second_weight, second_bias, head_weight, head_bias = params
    seg_count, length = (samples.shape[0], samples.shape[2])
    encoded = encode(samples, fourier)
    pre_first = jnp.dot(encoded, first_weight, preferred_element_type=jnp.float32) + first_bias
    act_first = jax.nn.silu(pre_first).astype(jnp.bfloat16)
    pre_second = jnp.dot(act_first, second_weight, preferred_element_type=jnp.float32) + second_bias
    act_second = jax.nn.silu(pre_second).astype(jnp.bfloat16)
    head_raw = (
        lax.dot_general(
            act_second, head_weight, (((1,), (1,)), ((), ())), preferred_element_type=jnp.float32
        )
        + head_bias
    )
    head_raw = head_raw.reshape(seg_count, length, 4)
    density = jax.nn.softplus(head_raw[..., 0])
    colour = jax.nn.sigmoid(head_raw[..., 1:])
    optical = density * samples[:, 3, :]
    inclusive = jnp.cumsum(optical, axis=1)
    enter_light = jnp.exp(optical - inclusive)
    leave_light = jnp.exp(-inclusive)
    weight = enter_light - leave_light
    seg_colour = jnp.sum(weight[..., None] * colour, axis=1)
    seg_log = -inclusive[:, -1]
    saved = (
        encoded,
        pre_first,
        act_first,
        pre_second,
        act_second,
        head_raw,
        colour,
        weight,
        leave_light,
    )
    return (seg_colour, seg_log, saved)


def backward(samples, params, saved, up_colour, up_log):
    first_weight, first_bias, second_weight, second_bias, head_weight, head_bias = params
    encoded, pre_first, act_first, pre_second, act_second, head_raw, colour, weight, leave_light = (
        saved
    )
    energy = jnp.sum(colour * up_colour[:, None, :], axis=-1)
    spent = weight * energy
    remaining = jnp.sum(spent, axis=1, keepdims=True) - jnp.cumsum(spent, axis=1)
    grad_optical = leave_light * energy - remaining - up_log[:, None]
    grad_density = grad_optical * samples[:, 3, :] * jax.nn.sigmoid(head_raw[..., 0])
    grad_tint = weight[..., None] * up_colour[:, None, :] * colour * (1.0 - colour)
    grad_raw = (
        jnp.concatenate([grad_density[..., None], grad_tint], axis=-1)
        .reshape(-1, 4)
        .astype(jnp.bfloat16)
    )
    grad_head = lax.dot_general(
        grad_raw, act_second, (((0,), (0,)), ((), ())), preferred_element_type=jnp.float32
    )
    grad_head_bias = jnp.sum(grad_raw.astype(jnp.float32), axis=0)
    back_second = jnp.dot(grad_raw, head_weight, preferred_element_type=jnp.float32)
    delta_second = (back_second * silu_slope(pre_second)).astype(jnp.bfloat16)
    grad_second = lax.dot_general(
        act_first, delta_second, (((0,), (0,)), ((), ())), preferred_element_type=jnp.float32
    )
    grad_second_bias = jnp.sum(delta_second.astype(jnp.float32), axis=0)
    back_first = lax.dot_general(
        delta_second, second_weight, (((1,), (1,)), ((), ())), preferred_element_type=jnp.float32
    )
    delta_first = (back_first * silu_slope(pre_first)).astype(jnp.bfloat16)
    grad_first = lax.dot_general(
        encoded, delta_first, (((0,), (0,)), ((), ())), preferred_element_type=jnp.float32
    )
    grad_first_bias = jnp.sum(delta_first.astype(jnp.float32), axis=0)
    return (grad_first, grad_second, grad_head, grad_first_bias, grad_second_bias, grad_head_bias)


def composite(seg_colour, seg_log, depth_rank, pixel_rows):
    before = (depth_rank[:, None, :] < depth_rank[:, :, None]).astype(jnp.float32)
    prefix = jnp.exp(jnp.sum(before * seg_log[:, None, :], axis=2))
    up_colour = prefix[..., None] * pixel_rows[:, None, :]
    shaded = prefix * jnp.sum(seg_colour * pixel_rows[:, None, :], axis=2)
    up_log = jnp.sum(before * shaded[:, :, None], axis=1)
    return (up_colour, up_log)


def per_device(
    positions,
    spacing,
    assign,
    depth_rank,
    pixel_grad,
    fourier,
    first_weight,
    first_bias,
    second_weight,
    second_bias,
    head_weight,
    head_bias,
):
    groups = lax.axis_size("space")
    ray_count = positions.shape[1]
    total = ray_count * SEGS
    capacity = 3 * total // (2 * groups)
    slot_count = capacity * groups
    owner = assign.reshape(total)
    member = (owner[:, None] == jnp.arange(groups, dtype=jnp.int32)[None, :]).astype(jnp.int32)
    earlier = jnp.cumsum(member, axis=0) - member
    within = jnp.sum(earlier * member, axis=1)
    target = owner * capacity + within
    dispatch = (target[:, None] == jnp.arange(slot_count, dtype=jnp.int32)[None, :]).astype(
        jnp.float32
    )
    seg_pos = jnp.transpose(positions.reshape(3, total, SEG_LEN), (1, 0, 2))
    seg_gap = spacing.reshape(total, 1, SEG_LEN)
    segments = jnp.concatenate([seg_pos, seg_gap], axis=1).reshape(total, 4 * SEG_LEN)
    outgoing = lax.dot_general(
        dispatch,
        segments,
        (((0,), (0,)), ((), ())),
        precision=lax.Precision.HIGHEST,
        preferred_element_type=jnp.float32,
    )
    outgoing = outgoing.reshape(groups, capacity, 4 * SEG_LEN)
    arrived = lax.all_to_all(outgoing, "space", split_axis=0, concat_axis=0, tiled=True)
    samples = arrived.reshape(slot_count, 4, SEG_LEN)
    params = tuple(
        (
            item[0]
            for item in (
                first_weight,
                first_bias,
                second_weight,
                second_bias,
                head_weight,
                head_bias,
            )
        )
    )
    seg_colour, seg_log, saved = network(samples, fourier, params)
    partials = jnp.concatenate([seg_colour.T, seg_log[None, :]], axis=0).reshape(
        4, groups, capacity
    )
    returned = lax.all_to_all(partials, "space", split_axis=1, concat_axis=1, tiled=True).reshape(
        4, slot_count
    )
    mine = lax.dot_general(
        dispatch,
        returned,
        (((1,), (1,)), ((), ())),
        precision=lax.Precision.HIGHEST,
        preferred_element_type=jnp.float32,
    )
    up_colour, up_log = composite(
        mine[:, :3].reshape(ray_count, SEGS, 3),
        mine[:, 3].reshape(ray_count, SEGS),
        depth_rank,
        pixel_grad.T,
    )
    upstream = jnp.concatenate([up_colour.reshape(total, 3), up_log.reshape(total, 1)], axis=1)
    sendback = lax.dot_general(
        upstream,
        dispatch,
        (((0,), (0,)), ((), ())),
        precision=lax.Precision.HIGHEST,
        preferred_element_type=jnp.float32,
    )
    sendback = sendback.reshape(4, groups, capacity)
    received = lax.all_to_all(sendback, "space", split_axis=1, concat_axis=1, tiled=True)
    received = received.reshape(4, slot_count).T
    totals = backward(samples, params, saved, received[:, :3], received[:, 3])
    grad_first, grad_second, grad_head, bias_first, bias_second, bias_head = totals
    replicas = lax.axis_size("ray")
    small = jnp.concatenate([grad_head.reshape(-1), bias_first, bias_second, bias_head], axis=0)
    if replicas & replicas - 1 == 0:
        position = lax.axis_index("ray")
        part_first, part_second = (grad_first, grad_second)
        distance = replicas // 2
        while distance >= 1:
            pairs = [(i, i ^ distance) for i in range(replicas)]
            half = part_first.shape[0] // 2
            upper = position // distance % 2
            keep_first = lax.dynamic_slice_in_dim(part_first, upper * half, half, 0)
            send_first = lax.dynamic_slice_in_dim(part_first, (1 - upper) * half, half, 0)
            keep_second = lax.dynamic_slice_in_dim(part_second, upper * half, half, 0)
            send_second = lax.dynamic_slice_in_dim(part_second, (1 - upper) * half, half, 0)
            got_first, got_second, got_small = lax.ppermute(
                (send_first, send_second, small), "ray", pairs
            )
            part_first = keep_first + got_first
            part_second = keep_second + got_second
            small = small + got_small
            distance //= 2
    else:
        part_first = lax.psum_scatter(grad_first, "ray", scatter_dimension=0, tiled=True)
        part_second = lax.psum_scatter(grad_second, "ray", scatter_dimension=0, tiled=True)
        small = lax.psum(small, "ray")
    heads = grad_head.size
    hidden = bias_first.shape[0]
    small_sums = (
        small[:heads].reshape(grad_head.shape),
        small[heads : heads + hidden],
        small[heads + hidden : heads + 2 * hidden],
        small[heads + 2 * hidden :],
    )
    return (
        part_first[None],
        part_second[None],
        small_sums[0][None],
        small_sums[1][None],
        small_sums[2][None],
        small_sums[3][None],
    )


def solution(mesh):
    placed = (
        P(None, ("space", "ray"), None),
        P(("space", "ray"), None),
        P(("space", "ray"), None, None),
        P(("space", "ray"), None),
        P(None, ("space", "ray")),
        P(),
        P("space", None, None),
        P("space", None),
        P("space", None, None),
        P("space", None),
        P("space", None, None),
        P("space", None),
    )
    return jax.shard_map(
        per_device,
        mesh=mesh,
        in_specs=placed,
        out_specs=(
            P("space", "ray", None),
            P("space", "ray", None),
            P("space", None, None),
            P("space", None),
            P("space", None),
            P("space", None),
        ),
        check_vma=False,
    )
```

profile of v0, /device:TPU:1, one launch (start us, length us, event | category | flops | bytes accessed | tf_op | source)
XLA Modules:
  0.0 90.0 jit_solution(858286756958283039)
XLA Ops:
  2.0 0.9 reshape.234
  4.0 0.9 fusion.21
  4.9 7.4 %all-to-all-start = ((f32[16,12,128]{2,1,0:T(8,128)}), f32[16,12,128]{2,1,0:T(8,128)S(1)}, u32[]{:S(2)}, u32[]{:S(2)}) async-start(f32[16,12,128]{2,1,0:T(8,128)} %fusion.21), calls=%async_computation | async-start | bytes 262144 | tf_op jit(solution)/shard_map/all_to_all | solution.py:179
  13.1 5.8 %all-to-all-done = f32[16,12,128]{2,1,0:T(8,128)S(1)} async-done(((f32[16,12,128]{2,1,0:T(8,128)}), f32[16,12,128]{2,1,0:T(8,128)S(1)}, u32[]{:S(2)}, u32[]{:S(2)}) %all-to-all-start) | async-done | bytes 98336 | tf_op jit(solution)/shard_map/all_to_all | solution.py:179
  19.2 0.9 %slice_reduce_fusion.2 = (f32[192,32]{1,0:T(8,128)S(1)}, f32[192,32]{1,0:T(8,128)S(1)}, f32[192,32]{1,0:T(8,128)S(1)}, f32[192,1,32]{2,1,0:T(1,128)S(1)}) fusion(f32[192,4,32]{2,1,0:T(4,128)S(1)} %reshape.237), kind=kLoop, calls=%fused_computation.61 | loop fusion | bytes 196608 | tf_op jit(solution)/shard_map/slice | solution.py:48
  20.4 5.6 %fusion.2 = (bf16[6144,128]{1,0:T(8,128)(2,1)S(1)}, bf16[6144,128]{1,0:T(8,128)(2,1)S(1)}) fusion(f32[128]{0:T(128)S(1)} %get-tuple-element.19, f32[6144]{0:T(1024)S(1)} %mul.319, f32[128]{0:T(128)S(1)} %get-tuple-element.20, f32[6144]{0:T(1024)S(1)} %mul.314, f32[128]{0:T(128)S(1)} %get-tuple-element.18, f32[6144]{0:T(1024)S(1)} %mul.309), kind=kLoop, calls=%fused_computation.15 | loop fusion | flops 36175872 | bytes 3220992 | tf_op jit(solution)/shard_map/convert.4
  26.1 4.7 %multiply_convert_fusion.1 = (bf16[6144,256]{1,0:T(8,128)(2,1)S(1)}, f32[6144,256]{1,0:T(8,128)}) fusion(f32[256]{0:T(256)S(1)} %bitcast.134, bf16[1,256,256]{2,1,0:T(8,128)(2,1)} %param.18, bf16[6144,128]{1,0:T(8,128)(2,1)S(1)} %get-tuple-element.13, bf16[6144,128]{1,0:T(8,128)(2,1)S(1)} %get-tuple-element.12), kind=kOutput, calls=%fused_computation.11 | convolution fusion | flops 821035008 | bytes 12715008 | tf_op jit(solution)/shard_map/dot_general | solution.py:61
  30.9 4.4 %multiply_convert_fusion = (bf16[6144,256]{1,0:T(8,128)(2,1)S(1)}, f32[6144,256]{1,0:T(8,128)}) fusion(f32[256]{0:T(256)S(1)} %bitcast.135, bf16[6144,256]{1,0:T(8,128)(2,1)S(1)} %get-tuple-element.21, bf16[1,256,256]{2,1,0:T(8,128)(2,1)S(1)} %copy-done), kind=kOutput, calls=%fused_computation.9 | convolution fusion | flops 814743552 | bytes 12715008 | tf_op jit(solution)/shard_map/dot_general | solution.py:63
  35.3 0.9 %convolution_add_fusion.2 = f32[6144,4]{0,1:T(4,128)S(1)} fusion(bf16[6144,256]{1,0:T(8,128)(2,1)S(1)} %get-tuple-element.23, f32[4]{0:T(128)S(1)} %bitcast.130, bf16[1,4,256]{2,1,0:T(4,128)(2,1)S(1)} %copy-done.6), kind=kOutput, calls=%fused_computation.6 | convolution fusion | flops 12607488 | bytes 3246096 | tf_op jit(solution)/shard_map/dot_general | solution.py:66
  36.2 0.9 %reshape.238 = f32[192,32,4]{1,0,2:T(8,128)} reshape(f32[6144,4]{0,1:T(4,128)S(1)} %convolution_add_fusion.2) | data formatting | bytes 196608 | tf_op jit(solution)/shard_map/reshape | solution.py:71
  37.1 0.9 slice.77
  38.4 1.2 %multiply_reduce_fusion.1 = f32[192,3]{0,1:T(4,128)S(1)} fusion(f32[192,32]{1,0:T(8,128)S(1)} %copy.60, f32[192,32,4]{1,0,2:T(8,128)} %reshape.238), kind=kLoop, calls=%fused_computation.48 | loop fusion | flops 91584 | bytes 100608 | tf_op jit(solution)/shard_map/reduce_sum | solution.py:79
  40.4 3.5 %all-to-all-start.1 = ((f32[4,16,12]{2,0,1:T(4,128)}), f32[4,16,12]{2,0,1:T(4,128)S(1)}, u32[]{:S(2)}, u32[]{:S(2)}) async-start(f32[4,16,12]{2,0,1:T(4,128)} %copy.61), calls=%async_computation.1 | async-start | bytes 65536 | tf_op jit(solution)/shard_map/all_to_all | solution.py:198
  45.4 4.7 %all-to-all-done.1 = f32[4,16,12]{2,0,1:T(4,128)S(1)} async-done(((f32[4,16,12]{2,0,1:T(4,128)}), f32[4,16,12]{2,0,1:T(4,128)S(1)}, u32[]{:S(2)}, u32[]{:S(2)}) %all-to-all-start.1) | async-done | bytes 3104 | tf_op jit(solution)/shard_map/all_to_all | solution.py:198
  54.9 3.7 %all-to-all-start.2 = ((f32[4,16,12]{2,0,1:T(4,128)}), f32[4,16,12]{2,0,1:T(4,128)S(1)}, u32[]{:S(2)}, u32[]{:S(2)}) async-start(f32[4,16,12]{2,0,1:T(4,128)} %copy.67), calls=%async_computation.2 | async-start | bytes 65536 | tf_op jit(solution)/shard_map/all_to_all | solution.py:223
  58.6 6.0 %all-to-all-done.2 = f32[4,16,12]{2,0,1:T(4,128)S(1)} async-done(((f32[4,16,12]{2,0,1:T(4,128)}), f32[4,16,12]{2,0,1:T(4,128)S(1)}, u32[]{:S(2)}, u32[]{:S(2)}) %all-to-all-start.2) | async-done | bytes 3104 | tf_op jit(solution)/shard_map/all_to_all | solution.py:223
  66.1 2.4 %multiply_reduce_fusion = (f32[192,32]{1,0:T(8,128)}, bf16[192,32,3]{1,0,2:T(8,128)(2,1)}) fusion(f32[192,3]{0,1:T(4,128)S(1)} %bitcast.126, f32[192,32,4]{1,0,2:T(8,128)} %reshape.238, f32[192,32]{1,0:T(8,128)S(1)} %copy.60), kind=kLoop, calls=%fused_computation.47 | loop fusion | flops 178176 | bytes 162048 | tf_op jit(solution)/shard_map/reduce_sum | solution.py:100
  68.5 1.0 %copy.69 = f32[192,32]{0,1:T(8,128)S(1)} copy(f32[192,32]{1,0:T(8,128)} %get-tuple-element.9) | data formatting | bytes 49152 | tf_op jit(solution)/shard_map/reduce_sum | solution.py:100
  69.9 1.1 %concatenate.35 = bf16[6144,3]{0,1:T(4,128)(2,1)S(1)} reshape(bf16[192,32,3]{1,0,2:T(8,128)(2,1)} %get-tuple-element.10) | data formatting | bytes 73728 | tf_op jit(solution)/shard_map/concatenate | solution.py:107
  71.7 5.2 %convert_reduce_fusion = (f32[256]{0:T(256)S(1)}, bf16[6144,256]{1,0:T(8,128)(2,1)S(1)}) fusion(f32[6144,256]{1,0:T(8,128)} %get-tuple-element.24, bf16[1,4,256]{2,1,0:T(4,128)(2,1)S(1)} %copy-done.6, bf16[6144,3]{0,1:T(4,128)(2,1)S(1)} %concatenate.35, bf16[6144,1]{0,1:T(2,128)(2,1)S(1)} %concatenate.34), kind=kOutput, calls=%fused_computation.7 | convolution fusion | flops 29982464 | bytes 9489408 | tf_op jit(solution)/shard_map/dot_general | solution.py:115
  76.9 1.0 %fusion.56 = f32[256,256]{1,0:T(8,128)S(1)} fusion(bf16[6144,256]{1,0:T(8,128)(2,1)S(1)} %copy-done.13, bf16[6144,256]{1,0:T(8,128)(2,1)S(1)} %get-tuple-element.26), kind=kOutput, calls=%fused_computation.126 | convolution fusion | flops 805306368 | bytes 6553600 | tf_op jit(solution)/shard_map/dot_general | solution.py:117
  78.0 2.8 %convert_reduce_fusion.1 = (f32[256]{0:T(256)S(1)}, bf16[6144,256]{1,0:T(8,128)(2,1)S(1)}) fusion(f32[6144,256]{1,0:T(8,128)S(1)} %bitcast.137, bf16[6144,256]{1,0:T(8,128)(2,1)S(1)} %get-tuple-element.26, bf16[1,256,256]{2,1,0:T(8,128)(2,1)S(1)} %copy-done), kind=kOutput, calls=%fused_computation.8 | convolution fusion | flops 822607616 | bytes 12715008 | tf_op jit(solution)/shard_map/dot_general | solution.py:121
  80.8 4.5 %collective-permute-start.2 = (f32[1540]{0:T(1024)S(1)}, f32[1540]{0:T(1024)S(1)}, u32[]{:S(2)}, u32[]{:S(2)}) collective-permute-start(f32[1540]{0:T(1024)S(1)} %pad_maximum_fusion.6), channel_id=1, source_target_pairs={{0,1},{1,0},{2,3},{3,2},{4,5},{5,4},{6,7},{7,6},{8,9},{9,8},{10,11... | collective-permute-start | bytes 18488 | tf_op jit(solution)/shard_map/ppermute | solution.py:241
  85.4 1.0 %fusion.12 = f32[256,256]{1,0:T(8,128)S(1)} fusion(bf16[6144,256]{1,0:T(8,128)(2,1)S(1)} %get-tuple-element.28, bf16[6144,128]{1,0:T(8,128)(2,1)S(1)} %copy-done.4, bf16[6144,128]{1,0:T(8,128)(2,1)S(1)} %copy-done.2), kind=kOutput, calls=%fused_computation.39 | convolution fusion | flops 811597824 | bytes 6553600 | tf_op jit(solution)/shard_map/dot_general | solution.py:125
  (110 shorter events, 17.4 us)
Async XLA Ops:
  0.6 30.2 %copy-start = (bf16[1,256,256]{2,1,0:T(8,128)(2,1)S(1)}, bf16[1,256,256]{2,1,0:T(8,128)(2,1)}, u32[]{:S(2)}) copy-start(bf16[1,256,256]{2,1,0:T(8,128)(2,1)} %param.20) | copy-start | bytes 393220
  1.8 24.3 %copy-start.10 = (f32[1,256]{1,0:T(1,128)S(1)}, f32[1,256]{1,0:T(1,128)}, u32[]{:S(2)}) copy-start(f32[1,256]{1,0:T(1,128)} %param.19) | copy-start | bytes 3076
  2.0 17.0 %copy-start.9 = (s32[128]{0:T(128)}, s32[128]{0:T(128)S(1)}, u32[]{:S(2)}) copy-start(s32[128]{0:T(128)S(1)} %multiply_add_fusion.2) | copy-start | bytes 1540
  4.9 14.1 %all-to-all-start = ((f32[16,12,128]{2,1,0:T(8,128)}), f32[16,12,128]{2,1,0:T(8,128)S(1)}, u32[]{:S(2)}, u32[]{:S(2)}) async-start(f32[16,12,128]{2,1,0:T(8,128)} %fusion.21), calls=%async_computation | async-start | bytes 262144 | tf_op jit(solution)/shard_map/all_to_all | solution.py:179
  26.1 4.8 %copy-start.1 = (bf16[6144,128]{1,0:T(8,128)(2,1)}, bf16[6144,128]{1,0:T(8,128)(2,1)S(1)}, u32[]{:S(2)}) copy-start(bf16[6144,128]{1,0:T(8,128)(2,1)S(1)} %get-tuple-element.12) | copy-start | bytes 4718596
  26.1 4.8 %copy-start.3 = (bf16[6144,128]{1,0:T(8,128)(2,1)}, bf16[6144,128]{1,0:T(8,128)(2,1)S(1)}, u32[]{:S(2)}) copy-start(bf16[6144,128]{1,0:T(8,128)(2,1)S(1)} %get-tuple-element.13) | copy-start | bytes 4718596
  26.1 4.8 %copy-start.11 = (f32[1,256]{1,0:T(1,128)S(1)}, f32[1,256]{1,0:T(1,128)}, u32[]{:S(2)}) copy-start(f32[1,256]{1,0:T(1,128)} %param.21) | copy-start | bytes 3076
  30.8 4.4 %copy-start.12 = (bf16[6144,256]{1,0:T(8,128)(2,1)}, bf16[6144,256]{1,0:T(8,128)(2,1)S(1)}, u32[]{:S(2)}) copy-start(bf16[6144,256]{1,0:T(8,128)(2,1)S(1)} %get-tuple-element.21) | copy-start | bytes 9437188
  30.9 4.4 %copy-start.6 = (bf16[1,4,256]{2,1,0:T(4,128)(2,1)S(1)}, bf16[1,4,256]{2,1,0:T(4,128)(2,1)}, u32[]{:S(2)}) copy-start(bf16[1,4,256]{2,1,0:T(4,128)(2,1)} %param.22) | copy-start | bytes 6148
  30.9 4.4 %copy-start.7 = (f32[1,4]{1,0:T(1,128)S(1)}, f32[1,4]{1,0:T(1,128)}, u32[]{:S(2)}) copy-start(f32[1,4]{1,0:T(1,128)} %param.23) | copy-start | bytes 52
  35.3 8.7 %copy-start.8 = (f32[3,16]{1,0:T(4,128)S(1)}, f32[3,16]{1,0:T(4,128)}, u32[]{:S(2)}) copy-start(f32[3,16]{1,0:T(4,128)} %param.16) | copy-start | bytes 580
  35.3 17.6 %copy-start.5 = (s32[16,8]{0,1:T(8,128)S(1)}, s32[16,8]{0,1:T(8,128)}, u32[]{:S(2)}) copy-start(s32[16,8]{0,1:T(8,128)} %param.15) | copy-start | bytes 1540
  40.4 9.7 %all-to-all-start.1 = ((f32[4,16,12]{2,0,1:T(4,128)}), f32[4,16,12]{2,0,1:T(4,128)S(1)}, u32[]{:S(2)}, u32[]{:S(2)}) async-start(f32[4,16,12]{2,0,1:T(4,128)} %copy.61), calls=%async_computation.1 | async-start | bytes 65536 | tf_op jit(solution)/shard_map/all_to_all | solution.py:198
  54.9 9.7 %all-to-all-start.2 = ((f32[4,16,12]{2,0,1:T(4,128)}), f32[4,16,12]{2,0,1:T(4,128)S(1)}, u32[]{:S(2)}, u32[]{:S(2)}) async-start(f32[4,16,12]{2,0,1:T(4,128)} %copy.67), calls=%async_computation.2 | async-start | bytes 65536 | tf_op jit(solution)/shard_map/all_to_all | solution.py:223
  71.0 7.0 %slice-start = ((s8[6291456]{0:T(1024)(128)(4,1)}), s8[4194304]{0:T(1024)(128)(4,1)S(1)}, s32[]{:S(2)}) async-start(s8[6291456]{0:T(1024)(128)(4,1)} %bitcast.136), calls=%async_computation.3 | async-start | bytes 8388608
  71.7 5.2 %copy-start.13 = (bf16[6144,256]{1,0:T(8,128)(2,1)S(1)}, bf16[6144,256]{1,0:T(8,128)(2,1)}, u32[]{:S(2)}) copy-start(bf16[6144,256]{1,0:T(8,128)(2,1)} %copy-done.12) | copy-start | bytes 9437188
  71.7 6.2 %slice-start.1 = ((s8[6291456]{0:T(1024)(128)(4,1)}), s8[2097152]{0:T(1024)(128)(4,1)S(1)}, s32[]{:S(2)}) async-start(s8[6291456]{0:T(1024)(128)(4,1)} %bitcast.136), calls=%async_computation.4 | async-start | bytes 4194304
  78.0 7.4 %copy-start.2 = (bf16[6144,128]{1,0:T(8,128)(2,1)S(1)}, bf16[6144,128]{1,0:T(8,128)(2,1)}, u32[]{:S(2)}) copy-start(bf16[6144,128]{1,0:T(8,128)(2,1)} %copy-done.1) | copy-start | bytes 4718596
  78.0 7.4 %copy-start.4 = (bf16[6144,128]{1,0:T(8,128)(2,1)S(1)}, bf16[6144,128]{1,0:T(8,128)(2,1)}, u32[]{:S(2)}) copy-start(bf16[6144,128]{1,0:T(8,128)(2,1)} %copy-done.3) | copy-start | bytes 4718596
  80.8 6.2 %collective-permute-start.2 = (f32[1540]{0:T(1024)S(1)}, f32[1540]{0:T(1024)S(1)}, u32[]{:S(2)}, u32[]{:S(2)}) collective-permute-start(f32[1540]{0:T(1024)S(1)} %pad_maximum_fusion.6), channel_id=1, source_target_pairs={{0,1},{1,0},{2,3},{3,2},{4,5},{5,4},{6,7},{7,6},{8,9},{9,8},{10,11... | collective-permute-start | bytes 18488 | tf_op jit(solution)/shard_map/ppermute | solution.py:241
  85.3 3.4 %collective-permute-start.1 = (f32[128,256]{1,0:T(8,128)S(1)}, f32[128,256]{1,0:T(8,128)S(1)}, u32[]{:S(2)}, u32[]{:S(2)}) collective-permute-start(f32[128,256]{1,0:T(8,128)S(1)} %constant_dynamic-slice_fusion.1), channel_id=1, source_target_pairs={{0,1},{1,0},{2,3},{3,2},{4,5},{5,4},{6,7},{7,6},{8,9},{9,8},{10,11... | collective-permute-start | bytes 393224 | tf_op jit(solution)/shard_map/ppermute | solution.py:241
  86.4 2.9 %collective-permute-start = (f32[128,256]{1,0:T(8,128)S(1)}, f32[128,256]{1,0:T(8,128)S(1)}, u32[]{:S(2)}, u32[]{:S(2)}) collective-permute-start(f32[128,256]{1,0:T(8,128)S(1)} %constant_dynamic-slice_fusion), channel_id=1, source_target_pairs={{0,1},{1,0},{2,3},{3,2},{4,5},{5,4},{6,7},{7,6},{8,9},{9,8},{10,11... | collective-permute-start | bytes 393224 | tf_op jit(solution)/shard_map/ppermute | solution.py:241
where the time goes:
time: 90.9 us; the launch traced here: 90 us
  matrix products  23.1 us (25%)
  starting transfers between devices  19.7 us (22%)
  local copies, waits for them, and re-layouts  17.7 us (19%)
  waiting for transfers between devices  16.6 us (18%)
  other arithmetic  11.7 us (13%)
  between operations  1.15 us (1%)
    all_to_all x1, starting transfers between devices, per_device(): lax.all_to_all(outgoing, 'space', split_axis=0, concat_axis=0, tiled=True)  7.41 us
    all_to_all x1, waiting for transfers between devices, per_device(): lax.all_to_all(sendback, 'space', split_axis=1, concat_axis=1, tiled=True)  6.02 us
    all_to_all x1, waiting for transfers between devices, per_device(): lax.all_to_all(outgoing, 'space', split_axis=0, concat_axis=0, tiled=True)  5.85 us
    another operation x2, other arithmetic  5.68 us
    dot_general x1, matrix products, backward(): jnp.dot(grad_raw, head_weight, preferred_element_type=jnp.float32)  5.17 us
    ppermute x3, starting transfers between devices, per_device(): lax.ppermute((send_first, send_second, small), 'ray', pairs)  5.1 us
    dot_general x1, matrix products, network(): jnp.dot(encoded, first_weight, preferred_element_type=jnp.float32)  4.73 us
    all_to_all x1, waiting for transfers between devices, per_device(): lax.all_to_all(partials, 'space', split_axis=1, concat_axis=1, tiled=True)  4.71 us
  transfers between devices with their start and end apart: 6, of which 3 were waited for; matrix products, arithmetic and copies ran while one was open for 6% of the time, Pallas kernels for 0%

commit v1 on v0

--- a/solution.py
+++ b/solution.py
@@ -2,6 +2,7 @@
 import jax.numpy as jnp
 from jax import lax
 from jax.sharding import PartitionSpec as P
+from jax.lax import all_to_all, axis_size
 
 SEG_LEN = 32
 SEGS = 8
@@ -220,7 +221,15 @@
         preferred_element_type=jnp.float32,
     )
     sendback = sendback.reshape(4, groups, capacity)
-    received = lax.all_to_all(sendback, "space", split_axis=1, concat_axis=1, tiled=True)
+    received = jnp.concatenate(
+        all_to_all(
+            jnp.stack(jnp.split(sendback, axis_size("space"), axis=1)),
+            axis_name="space",
+            split_axis=0,
+            concat_axis=0,
+        ),
+        axis=1,
+    )
     received = received.reshape(4, slot_count).T
     totals = backward(samples, params, saved, received[:, :3], received[:, 3])
     grad_first, grad_second, grad_head, bias_first, bias_second, bias_head = totals

time: 90.9 us -> 98.4 us (1.083)
  local copies, waits for them, and re-layouts: 17.7 us -> 26.4 us
  matrix products: 23.1 us -> 22 us
    unnamed x36 -> x53, local copies, waits for them, and re-layouts: 1.02 us -> 9.7 us
    another operation x1 -> x3, local copies, waits for them, and re-layouts: 0.11 us -> 1.54 us  [the longest x1 0.84 us: per_device(): received = received.reshape(4, slot_count).T]
    dot_general x1, matrix products: 4.73 us -> 3.62 us  [network(): jnp.dot(encoded, first_weight, preferred_element_type=jnp.float32)]
where the time goes in v1:
time: 98.4 us; the launch traced here: 97.6 us
  local copies, waits for them, and re-layouts  26.4 us (27%)
  matrix products  22 us (22%)
  starting transfers between devices  19.7 us (20%)
  waiting for transfers between devices  16.6 us (17%)
  other arithmetic  11.7 us (12%)
  between operations  1.18 us (1%)
    unnamed x53, local copies, waits for them, and re-layouts  9.7 us
    all_to_all x1, starting transfers between devices, per_device(): lax.all_to_all(outgoing, 'space', split_axis=0, concat_axis=0, tiled=True)  7.42 us
    all_to_all x1, waiting for transfers between devices, per_device(): all_to_all(jnp.stack(jnp.split(sendback, axis_size('space'), axis=1)), ax...  6.02 us
    all_to_all x1, waiting for transfers between devices, per_device(): lax.all_to_all(outgoing, 'space', split_axis=0, concat_axis=0, tiled=True)  5.85 us
    another operation x2, other arithmetic  5.68 us
    dot_general x1, matrix products, backward(): jnp.dot(grad_raw, head_weight, preferred_element_type=jnp.float32)  5.18 us
    ppermute x3, starting transfers between devices, per_device(): lax.ppermute((send_first, send_second, small), 'ray', pairs)  5.11 us
    all_to_all x1, waiting for transfers between devices, per_device(): lax.all_to_all(partials, 'space', split_axis=1, concat_axis=1, tiled=True)  4.71 us
  transfers between devices with their start and end apart: 6, of which 3 were waited for; matrix products, arithmetic and copies ran while one was open for 6% of the time, Pallas kernels for 0%

profile of v1, /device:TPU:1, one launch (start us, length us, event | category | flops | bytes accessed | tf_op | source)
XLA Modules:
  0.0 97.6 jit_solution(4750769835178546444)
XLA Ops:
  2.0 0.9 reshape.234
  4.0 0.9 fusion.21
  4.9 7.4 %all-to-all-start = ((f32[16,12,128]{2,1,0:T(8,128)}), f32[16,12,128]{2,1,0:T(8,128)S(1)}, u32[]{:S(2)}, u32[]{:S(2)}) async-start(f32[16,12,128]{2,1,0:T(8,128)} %fusion.21), calls=%async_computation | async-start | bytes 262144 | tf_op jit(solution)/shard_map/all_to_all | solution.py:180
  13.1 5.8 %all-to-all-done = f32[16,12,128]{2,1,0:T(8,128)S(1)} async-done(((f32[16,12,128]{2,1,0:T(8,128)}), f32[16,12,128]{2,1,0:T(8,128)S(1)}, u32[]{:S(2)}, u32[]{:S(2)}) %all-to-all-start) | async-done | bytes 98336 | tf_op jit(solution)/shard_map/all_to_all | solution.py:180
  19.2 0.9 slice_reduce_fusion.2
  20.4 5.6 %fusion.2 = (bf16[6144,128]{1,0:T(8,128)(2,1)S(1)}, bf16[6144,128]{1,0:T(8,128)(2,1)S(1)}) fusion(f32[128]{0:T(128)S(1)} %get-tuple-element.35, f32[6144]{0:T(1024)S(1)} %mul.319, f32[128]{0:T(128)S(1)} %get-tuple-element.36, f32[6144]{0:T(1024)S(1)} %mul.314, f32[128]{0:T(128)S(1)} %get-tuple-element.34, f32[6144]{0:T(1024)S(1)} %mul.309), kind=kLoop, calls=%fused_computation.15 | loop fusion | flops 36175872 | bytes 3220992 | tf_op jit(solution)/shard_map/convert.4
  26.1 3.6 %multiply_convert_fusion.1 = (bf16[6144,256]{1,0:T(8,128)(2,1)S(1)}, f32[6144,256]{1,0:T(8,128)}) fusion(f32[256]{0:T(256)S(1)} %bitcast.172, bf16[1,256,256]{2,1,0:T(8,128)(2,1)S(1)} %copy-done.10, bf16[6144,128]{1,0:T(8,128)(2,1)S(1)} %get-tuple-element.13, bf16[6144,128]{1,0:T(8,128)(2,1)S(1)} %get-tuple-element.12), kind=kOutput, calls=%fused_computation.11 | convolution fusion | flops 821035008 | bytes 12715008 | tf_op jit(solution)/shard_map/dot_general | solution.py:62
  29.8 4.4 %multiply_convert_fusion = (bf16[6144,256]{1,0:T(8,128)(2,1)S(1)}, f32[6144,256]{1,0:T(8,128)}) fusion(f32[256]{0:T(256)S(1)} %bitcast.173, bf16[6144,256]{1,0:T(8,128)(2,1)S(1)} %get-tuple-element.37, bf16[1,256,256]{2,1,0:T(8,128)(2,1)S(1)} %copy-done), kind=kOutput, calls=%fused_computation.9 | convolution fusion | flops 814743552 | bytes 12715008 | tf_op jit(solution)/shard_map/dot_general | solution.py:64
  34.2 0.9 convolution_add_fusion.2
  35.1 0.9 reshape.238
  36.0 0.9 slice.77
  37.3 1.2 %multiply_reduce_fusion.1 = f32[192,3]{0,1:T(4,128)S(1)} fusion(f32[192,32]{1,0:T(8,128)S(1)} %copy.76, f32[192,32,4]{1,0,2:T(8,128)} %reshape.238), kind=kLoop, calls=%fused_computation.48 | loop fusion | flops 91584 | bytes 100608 | tf_op jit(solution)/shard_map/reduce_sum | solution.py:80
  39.3 3.5 %all-to-all-start.1 = ((f32[4,16,12]{2,0,1:T(4,128)}), f32[4,16,12]{2,0,1:T(4,128)S(1)}, u32[]{:S(2)}, u32[]{:S(2)}) async-start(f32[4,16,12]{2,0,1:T(4,128)} %copy.77), calls=%async_computation.1 | async-start | bytes 65536 | tf_op jit(solution)/shard_map/all_to_all | solution.py:199
  44.3 4.7 %all-to-all-done.1 = f32[4,16,12]{2,0,1:T(4,128)S(1)} async-done(((f32[4,16,12]{2,0,1:T(4,128)}), f32[4,16,12]{2,0,1:T(4,128)S(1)}, u32[]{:S(2)}, u32[]{:S(2)}) %all-to-all-start.1) | async-done | bytes 3104 | tf_op jit(solution)/shard_map/all_to_all | solution.py:199
  62.5 3.7 %all-to-all-start.2 = ((f32[16,4,1,12]{3,1,2,0:T(4,128)}), f32[16,4,1,12]{3,1,2,0:T(4,128)S(1)}, u32[]{:S(2)}, u32[]{:S(2)}) async-start(f32[16,4,1,12]{3,1,2,0:T(4,128)} %constant_dynamic-update-slice_fusion), calls=%async_computation.2 | async-start | bytes 65536 | tf_op jit(solution)/shard_map/all_to_all | solution.py:225
  66.2 6.0 %all-to-all-done.2 = f32[16,4,1,12]{3,1,2,0:T(4,128)S(1)} async-done(((f32[16,4,1,12]{3,1,2,0:T(4,128)}), f32[16,4,1,12]{3,1,2,0:T(4,128)S(1)}, u32[]{:S(2)}, u32[]{:S(2)}) %all-to-all-start.2) | async-done | bytes 3104 | tf_op jit(solution)/shard_map/all_to_all | solution.py:225
  73.7 2.4 %multiply_reduce_fusion = (f32[192,32]{1,0:T(8,128)}, bf16[192,32,3]{1,0,2:T(8,128)(2,1)}) fusion(f32[192,3]{0,1:T(4,128)S(1)} %bitcast.148, f32[192,32,4]{1,0,2:T(8,128)} %reshape.238, f32[192,32]{1,0:T(8,128)S(1)} %copy.76), kind=kLoop, calls=%fused_computation.47 | loop fusion | flops 178176 | bytes 162048 | tf_op jit(solution)/shard_map/reduce_sum | solution.py:101
  76.1 1.0 copy.84
  77.5 1.1 %concatenate.35 = bf16[6144,3]{0,1:T(4,128)(2,1)S(1)} reshape(bf16[192,32,3]{1,0,2:T(8,128)(2,1)} %get-tuple-element.10) | data formatting | bytes 73728 | tf_op jit(solution)/shard_map/concatenate | solution.py:108
  79.3 5.2 %convert_reduce_fusion = (f32[256]{0:T(256)S(1)}, bf16[6144,256]{1,0:T(8,128)(2,1)S(1)}) fusion(f32[6144,256]{1,0:T(8,128)} %get-tuple-element.40, bf16[1,4,256]{2,1,0:T(4,128)(2,1)S(1)} %copy-done.6, bf16[6144,3]{0,1:T(4,128)(2,1)S(1)} %concatenate.35, bf16[6144,1]{0,1:T(2,128)(2,1)S(1)} %concatenate.34), kind=kOutput, calls=%fused_computation.7 | convolution fusion | flops 29982464 | bytes 9489408 | tf_op jit(solution)/shard_map/dot_general | solution.py:116
  84.5 1.0 %fusion.57 = f32[256,256]{1,0:T(8,128)S(1)} fusion(bf16[6144,256]{1,0:T(8,128)(2,1)S(1)} %copy-done.14, bf16[6144,256]{1,0:T(8,128)(2,1)S(1)} %get-tuple-element.42), kind=kOutput, calls=%fused_computation.143 | convolution fusion | flops 805306368 | bytes 6553600 | tf_op jit(solution)/shard_map/dot_general | solution.py:118
  85.6 2.7 %convert_reduce_fusion.1 = (f32[256]{0:T(256)S(1)}, bf16[6144,256]{1,0:T(8,128)(2,1)S(1)}) fusion(f32[6144,256]{1,0:T(8,128)S(1)} %bitcast.175, bf16[6144,256]{1,0:T(8,128)(2,1)S(1)} %get-tuple-element.42, bf16[1,256,256]{2,1,0:T(8,128)(2,1)S(1)} %copy-done), kind=kOutput, calls=%fused_computation.8 | convolution fusion | flops 822607616 | bytes 12715008 | tf_op jit(solution)/shard_map/dot_general | solution.py:122
  88.3 4.5 %collective-permute-start.2 = (f32[1540]{0:T(1024)S(1)}, f32[1540]{0:T(1024)S(1)}, u32[]{:S(2)}, u32[]{:S(2)}) collective-permute-start(f32[1540]{0:T(1024)S(1)} %pad_maximum_fusion.6), channel_id=1, source_target_pairs={{0,1},{1,0},{2,3},{3,2},{4,5},{5,4},{6,7},{7,6},{8,9},{9,8},{10,11... | collective-permute-start | bytes 18488 | tf_op jit(solution)/shard_map/ppermute | solution.py:250
  92.9 1.0 %fusion.12 = f32[256,256]{1,0:T(8,128)S(1)} fusion(bf16[6144,256]{1,0:T(8,128)(2,1)S(1)} %get-tuple-element.44, bf16[6144,128]{1,0:T(8,128)(2,1)S(1)} %copy-done.4, bf16[6144,128]{1,0:T(8,128)(2,1)S(1)} %copy-done.2), kind=kOutput, calls=%fused_computation.39 | convolution fusion | flops 811597824 | bytes 6553600 | tf_op jit(solution)/shard_map/dot_general | solution.py:126
  (128 shorter events, 26.1 us)
Async XLA Ops:
  0.6 29.1 %copy-start = (bf16[1,256,256]{2,1,0:T(8,128)(2,1)S(1)}, bf16[1,256,256]{2,1,0:T(8,128)(2,1)}, u32[]{:S(2)}) copy-start(bf16[1,256,256]{2,1,0:T(8,128)(2,1)} %param.20) | copy-start | bytes 393220
  1.8 24.3 %copy-start.10 = (bf16[1,256,256]{2,1,0:T(8,128)(2,1)S(1)}, bf16[1,256,256]{2,1,0:T(8,128)(2,1)}, u32[]{:S(2)}) copy-start(bf16[1,256,256]{2,1,0:T(8,128)(2,1)} %param.18) | copy-start | bytes 393220
  1.8 24.3 %copy-start.11 = (f32[1,256]{1,0:T(1,128)S(1)}, f32[1,256]{1,0:T(1,128)}, u32[]{:S(2)}) copy-start(f32[1,256]{1,0:T(1,128)} %param.19) | copy-start | bytes 3076
  2.0 17.0 %copy-start.9 = (s32[128]{0:T(128)}, s32[128]{0:T(128)S(1)}, u32[]{:S(2)}) copy-start(s32[128]{0:T(128)S(1)} %multiply_add_fusion.2) | copy-start | bytes 1540
  4.9 14.1 %all-to-all-start = ((f32[16,12,128]{2,1,0:T(8,128)}), f32[16,12,128]{2,1,0:T(8,128)S(1)}, u32[]{:S(2)}, u32[]{:S(2)}) async-start(f32[16,12,128]{2,1,0:T(8,128)} %fusion.21), calls=%async_computation | async-start | bytes 262144 | tf_op jit(solution)/shard_map/all_to_all | solution.py:180
  26.1 3.7 %copy-start.1 = (bf16[6144,128]{1,0:T(8,128)(2,1)}, bf16[6144,128]{1,0:T(8,128)(2,1)S(1)}, u32[]{:S(2)}) copy-start(bf16[6144,128]{1,0:T(8,128)(2,1)S(1)} %get-tuple-element.12) | copy-start | bytes 4718596
  26.1 3.7 %copy-start.3 = (bf16[6144,128]{1,0:T(8,128)(2,1)}, bf16[6144,128]{1,0:T(8,128)(2,1)S(1)}, u32[]{:S(2)}) copy-start(bf16[6144,128]{1,0:T(8,128)(2,1)S(1)} %get-tuple-element.13) | copy-start | bytes 4718596
  26.1 3.6 %copy-start.12 = (f32[1,256]{1,0:T(1,128)S(1)}, f32[1,256]{1,0:T(1,128)}, u32[]{:S(2)}) copy-start(f32[1,256]{1,0:T(1,128)} %param.21) | copy-start | bytes 3076
  29.7 4.4 %copy-start.13 = (bf16[6144,256]{1,0:T(8,128)(2,1)}, bf16[6144,256]{1,0:T(8,128)(2,1)S(1)}, u32[]{:S(2)}) copy-start(bf16[6144,256]{1,0:T(8,128)(2,1)S(1)} %get-tuple-element.37) | copy-start | bytes 9437188
  29.8 4.4 %copy-start.6 = (bf16[1,4,256]{2,1,0:T(4,128)(2,1)S(1)}, bf16[1,4,256]{2,1,0:T(4,128)(2,1)}, u32[]{:S(2)}) copy-start(bf16[1,4,256]{2,1,0:T(4,128)(2,1)} %param.22) | copy-start | bytes 6148
  29.8 4.4 %copy-start.7 = (f32[1,4]{1,0:T(1,128)S(1)}, f32[1,4]{1,0:T(1,128)}, u32[]{:S(2)}) copy-start(f32[1,4]{1,0:T(1,128)} %param.23) | copy-start | bytes 52
  34.2 8.7 %copy-start.8 = (f32[3,16]{1,0:T(4,128)S(1)}, f32[3,16]{1,0:T(4,128)}, u32[]{:S(2)}) copy-start(f32[3,16]{1,0:T(4,128)} %param.16) | copy-start | bytes 580
  34.2 17.6 %copy-start.5 = (s32[16,8]{0,1:T(8,128)S(1)}, s32[16,8]{0,1:T(8,128)}, u32[]{:S(2)}) copy-start(s32[16,8]{0,1:T(8,128)} %param.15) | copy-start | bytes 1540
  39.3 9.7 %all-to-all-start.1 = ((f32[4,16,12]{2,0,1:T(4,128)}), f32[4,16,12]{2,0,1:T(4,128)S(1)}, u32[]{:S(2)}, u32[]{:S(2)}) async-start(f32[4,16,12]{2,0,1:T(4,128)} %copy.77), calls=%async_computation.1 | async-start | bytes 65536 | tf_op jit(solution)/shard_map/all_to_all | solution.py:199
  62.5 9.7 %all-to-all-start.2 = ((f32[16,4,1,12]{3,1,2,0:T(4,128)}), f32[16,4,1,12]{3,1,2,0:T(4,128)S(1)}, u32[]{:S(2)}, u32[]{:S(2)}) async-start(f32[16,4,1,12]{3,1,2,0:T(4,128)} %constant_dynamic-update-slice_fusion), calls=%async_computation.2 | async-start | bytes 65536 | tf_op jit(solution)/shard_map/all_to_all | solution.py:225
  78.6 6.9 %slice-start = ((s8[6291456]{0:T(1024)(128)(4,1)}), s8[4194304]{0:T(1024)(128)(4,1)S(1)}, s32[]{:S(2)}) async-start(s8[6291456]{0:T(1024)(128)(4,1)} %bitcast.174), calls=%async_computation.3 | async-start | bytes 8388608
  79.3 5.2 %copy-start.14 = (bf16[6144,256]{1,0:T(8,128)(2,1)S(1)}, bf16[6144,256]{1,0:T(8,128)(2,1)}, u32[]{:S(2)}) copy-start(bf16[6144,256]{1,0:T(8,128)(2,1)} %copy-done.13) | copy-start | bytes 9437188
  79.3 6.2 %slice-start.1 = ((s8[6291456]{0:T(1024)(128)(4,1)}), s8[2097152]{0:T(1024)(128)(4,1)S(1)}, s32[]{:S(2)}) async-start(s8[6291456]{0:T(1024)(128)(4,1)} %bitcast.174), calls=%async_computation.4 | async-start | bytes 4194304
  85.5 7.3 %copy-start.2 = (bf16[6144,128]{1,0:T(8,128)(2,1)S(1)}, bf16[6144,128]{1,0:T(8,128)(2,1)}, u32[]{:S(2)}) copy-start(bf16[6144,128]{1,0:T(8,128)(2,1)} %copy-done.1) | copy-start | bytes 4718596
  85.5 7.3 %copy-start.4 = (bf16[6144,128]{1,0:T(8,128)(2,1)S(1)}, bf16[6144,128]{1,0:T(8,128)(2,1)}, u32[]{:S(2)}) copy-start(bf16[6144,128]{1,0:T(8,128)(2,1)} %copy-done.3) | copy-start | bytes 4718596
  88.3 6.2 %collective-permute-start.2 = (f32[1540]{0:T(1024)S(1)}, f32[1540]{0:T(1024)S(1)}, u32[]{:S(2)}, u32[]{:S(2)}) collective-permute-start(f32[1540]{0:T(1024)S(1)} %pad_maximum_fusion.6), channel_id=1, source_target_pairs={{0,1},{1,0},{2,3},{3,2},{4,5},{5,4},{6,7},{7,6},{8,9},{9,8},{10,11... | collective-permute-start | bytes 18488 | tf_op jit(solution)/shard_map/ppermute | solution.py:250
  92.8 3.4 %collective-permute-start.1 = (f32[128,256]{1,0:T(8,128)S(1)}, f32[128,256]{1,0:T(8,128)S(1)}, u32[]{:S(2)}, u32[]{:S(2)}) collective-permute-start(f32[128,256]{1,0:T(8,128)S(1)} %constant_dynamic-slice_fusion.1), channel_id=1, source_target_pairs={{0,1},{1,0},{2,3},{3,2},{4,5},{5,4},{6,7},{7,6},{8,9},{9,8},{10,11... | collective-permute-start | bytes 393224 | tf_op jit(solution)/shard_map/ppermute | solution.py:250
  94.0 2.9 %collective-permute-start = (f32[128,256]{1,0:T(8,128)S(1)}, f32[128,256]{1,0:T(8,128)S(1)}, u32[]{:S(2)}, u32[]{:S(2)}) collective-permute-start(f32[128,256]{1,0:T(8,128)S(1)} %constant_dynamic-slice_fusion), channel_id=1, source_target_pairs={{0,1},{1,0},{2,3},{3,2},{4,5},{5,4},{6,7},{7,6},{8,9},{9,8},{10,11... | collective-permute-start | bytes 393224 | tf_op jit(solution)/shard_map/ppermute | solution.py:250
